TPU v7x, 256 devices: a whole 4x4x8 slice. The times are simulated.
256 devices in a mesh: dp: 32 (over x, y, z_lo), tensor: 8 (over z_hi, core).
Axes of the slice: x: 4, y: 4, z: 8 (z_hi: 4, z_lo: 2; z = z_hi * 2 + z_lo), core: 2. Of those that a mesh axis runs over, the one named last changes fastest.
Arguments:
- arrivals: bfloat16 [32768, 2048], P('dp', 'tensor')
- deal: int32 [32, 32], P('dp'), may hold values from 0 to 1023, as said below
- seg_ids: int32 [32, 1024], P('dp'), may hold values from 0 to 7, never falling along the last dimension, each value on 1 to 512 neighbouring positions
- page_table: int32 [32, 8], P('dp'), may hold values from 0 to 7, each once within a row
- attn_gain: float32 [2048], replicated, may hold values from 0.1 to 1.9
- w_query: bfloat16 [2048, 1024], P(None, 'tensor'), may hold values from -0.125 to 0.125
- w_keyval: bfloat16 [2048, 512], replicated, may hold values from -0.125 to 0.125
- query_gain: float32 [64], replicated, may hold values from 0.1 to 1.9
- key_gain: float32 [64], replicated, may hold values from 0.1 to 1.9
- w_out: bfloat16 [1024, 2048], P('tensor'), may hold values from -0.1875 to 0.1875
- ffn_gain: float32 [2048], replicated, may hold values from 0.1 to 1.9
- w_gate: bfloat16 [2048, 5120], P(None, 'tensor'), may hold values from -0.125 to 0.125
- w_up: bfloat16 [2048, 5120], P(None, 'tensor'), may hold values from -0.125 to 0.125
- w_down: bfloat16 [5120, 2048], P('tensor'), may hold values from -0.078125 to 0.078125
Outputs:
- result: bfloat16 [32768, 2048], P('dp', 'tensor')
- kv_pages: bfloat16 [256, 128, 512], P('dp', None, 'tensor')
Inputs may be any that keep to these rules, and one draw needn't show every extreme that they name: deal[s, k] = g * 32 + j sends unit k of arrival block s to unit j of group g; every value occurs once; the units of one arrival block go to exactly 16 groups, 2 units to each. `seg_ids`: each row never falls; one prompt is one run of equal numbers. `page_table`: each row holds every page number once.
All inputs are finite; a program needn't handle non-finite values.
Results may differ from a plain program's by a relative error of at most 0.019.
Values may be sent and summed in bfloat16 or wider, within the bound.
No kernel may reach another device: no remote copies, remote signals or barrier semaphores. Data moves between devices by JAX's collectives and lax.ppermute only.
A program may use at most 128 MiB of HBM per device.

v0:
```python
import math
import jax
import jax.numpy as jnp
from jax import lax
from jax.sharding import PartitionSpec as P

HEAD = 64
KVH = 4
MOST = 2
PAGE = 128
EPS = 1e-06
THETA = 10000.0
BLOCK_ROWS = 512


def rms_scale(values, gain):
    values = values.astype(jnp.float32)
    mean_sq = jnp.mean(values * values, axis=-1, keepdims=True)
    return values * lax.rsqrt(mean_sq + EPS) * gain


def rope_tables(positions, width):
    half = width // 2
    inverse = THETA ** (-jnp.arange(half, dtype=jnp.float32) * 2.0 / width)
    angles = positions.astype(jnp.float32)[:, None] * inverse[None, :]
    return (jnp.cos(angles), jnp.sin(angles))


def rotate(values, cosine, sine):
    half = values.shape[-1] // 2
    first = values[..., :half]
    second = values[..., half:]
    cos_b = cosine[:, None, :]
    sin_b = sine[:, None, :]
    return jnp.concatenate(
        [first * cos_b - second * sin_b, second * cos_b + first * sin_b], axis=-1
    )


def segment_starts(seg_row):
    count = seg_row.shape[0]
    index = jnp.arange(count, dtype=jnp.int32)
    prior = jnp.concatenate([seg_row[:1] - 1, seg_row[:-1]])
    marks = jnp.where(seg_row != prior, index, 0)
    return lax.cummax(marks, axis=0)


def on_device(
    arrivals,
    deal,
    seg_ids,
    page_table,
    attn_gain,
    w_query,
    w_keyval,
    query_gain,
    key_gain,
    w_out,
    ffn_gain,
    w_gate,
    w_up,
    w_down,
):
    groups = lax.axis_size("dp")
    shards = lax.axis_size("tensor")
    tensor_rank = lax.axis_index("tensor")
    tok_grp = arrivals.shape[0]
    feat_part = arrivals.shape[1]
    units = deal.shape[1]
    unit_rows = tok_grp // units
    slot_count = groups * MOST
    width = unit_rows * feat_part
    dest_row = deal[0]
    target = dest_row // units
    position = dest_row % units
    unit_index = jnp.arange(units, dtype=jnp.int32)
    earlier = unit_index[:, None] > unit_index[None, :]
    same_target = target[:, None] == target[None, :]
    rank = jnp.sum(jnp.logical_and(earlier, same_target), axis=1)
    slot = target * MOST + rank
    send_hot = slot[None, :] == jnp.arange(slot_count, dtype=jnp.int32)[:, None]
    filled = jnp.any(send_hot, axis=1)
    slot_pos = jnp.where(filled, jnp.sum(jnp.where(send_hot, position[None, :], 0), axis=1), -1)
    send_matrix = send_hot.astype(jnp.bfloat16)
    packed = jnp.dot(
        send_matrix, arrivals.reshape(units, width), preferred_element_type=jnp.float32
    ).astype(jnp.bfloat16)
    received, recv_pos = (
        lax.all_to_all(
            packed.reshape(groups, MOST, width), "dp", split_axis=0, concat_axis=0, tiled=True
        ),
        lax.all_to_all(
            slot_pos.reshape(groups, MOST), "dp", split_axis=0, concat_axis=0, tiled=True
        ),
    )
    recv_matrix = (recv_pos.reshape(-1)[None, :] == unit_index[:, None]).astype(jnp.bfloat16)
    grouped = jnp.dot(
        recv_matrix, received.reshape(slot_count, width), preferred_element_type=jnp.float32
    ).astype(jnp.bfloat16)
    grouped = grouped.reshape(tok_grp, feat_part)
    full = lax.all_gather(grouped, "tensor", axis=1, tiled=True)
    normed = rms_scale(full, attn_gain).astype(jnp.bfloat16)
    seg_row = seg_ids[0]
    starts = segment_starts(seg_row)
    index = jnp.arange(tok_grp, dtype=jnp.int32)
    cosine, sine = rope_tables(index - starts, HEAD)
    q_heads = w_query.shape[1] // HEAD
    q_raw = jnp.dot(normed, w_query, preferred_element_type=jnp.float32).reshape(
        tok_grp, q_heads, HEAD
    )
    queries = rotate(rms_scale(q_raw, query_gain), cosine, sine).astype(jnp.bfloat16)
    kv_heads = max(1, KVH // shards)
    kv_first = tensor_rank * KVH // shards
    kv_weight = lax.dynamic_slice_in_dim(w_keyval, kv_first * 2 * HEAD, kv_heads * 2 * HEAD, 1)
    kv_raw = jnp.dot(normed, kv_weight, preferred_element_type=jnp.float32).reshape(
        tok_grp, kv_heads, 2, HEAD
    )
    keys = rotate(rms_scale(kv_raw[:, :, 0], key_gain), cosine, sine).astype(jnp.bfloat16)
    values = kv_raw[:, :, 1].astype(jnp.bfloat16)
    stacked = jnp.stack([keys, values], axis=2).reshape(tok_grp, kv_heads * 2 * HEAD)
    cache_cols = 2 * KVH * HEAD // shards
    offset = tensor_rank * cache_cols - kv_first * 2 * HEAD
    own_cache = lax.dynamic_slice_in_dim(stacked, offset, cache_cols, 1)
    pages = own_cache.reshape(tok_grp // PAGE, PAGE, cache_cols)
    kv_pages = jnp.zeros_like(pages).at[page_table[0]].set(pages)
    share = q_heads // kv_heads
    grouped_q = queries.reshape(tok_grp, kv_heads, share, HEAD)
    scale = 1.0 / math.sqrt(HEAD)
    block = min(BLOCK_ROWS, tok_grp)
    outputs = []
    for first in range(0, tok_grp, block):
        last = first + block
        scores = (
            jnp.einsum(
                "ikgd,jkd->kgij",
                grouped_q[first:last],
                keys[:last],
                preferred_element_type=jnp.float32,
            )
            * scale
        )
        query_rows = index[first:last]
        allowed = jnp.logical_and(
            query_rows[:, None] >= index[None, :last],
            starts[first:last][:, None] <= index[None, :last],
        )
        weights = jnp.where(allowed, jnp.exp(scores), 0.0)
        probs = (weights / jnp.sum(weights, axis=-1, keepdims=True)).astype(jnp.bfloat16)
        mixed = jnp.einsum(
            "kgij,jkd->ikgd", probs, values[:last], preferred_element_type=jnp.float32
        )
        outputs.append(mixed.astype(jnp.bfloat16).reshape(block, q_heads * HEAD))
    attended = jnp.concatenate(outputs, axis=0)
    attn_sum = lax.psum(
        jnp.dot(attended, w_out, preferred_element_type=jnp.float32).astype(jnp.bfloat16), "tensor"
    ).astype(jnp.float32)
    middle = (full.astype(jnp.float32) + attn_sum).astype(jnp.bfloat16)
    ffn_in = rms_scale(middle, ffn_gain).astype(jnp.bfloat16)
    gate = jnp.dot(ffn_in, w_gate, preferred_element_type=jnp.float32)
    upper = jnp.dot(ffn_in, w_up, preferred_element_type=jnp.float32)
    hidden = (jax.nn.silu(gate) * upper).astype(jnp.bfloat16)
    ffn_part = lax.psum_scatter(
        jnp.dot(hidden, w_down, preferred_element_type=jnp.float32).astype(jnp.bfloat16),
        "tensor",
        scatter_dimension=1,
        tiled=True,
    ).astype(jnp.float32)
    own_cols = lax.dynamic_slice_in_dim(middle, tensor_rank * feat_part, feat_part, 1)
    combined = (own_cols.astype(jnp.float32) + ffn_part).astype(jnp.bfloat16)
    back = jnp.dot(
        recv_matrix.T, combined.reshape(units, width), preferred_element_type=jnp.float32
    ).astype(jnp.bfloat16)
    returned = lax.all_to_all(
        back.reshape(groups, MOST, width), "dp", split_axis=0, concat_axis=0, tiled=True
    )
    result = jnp.dot(
        send_matrix.T, returned.reshape(slot_count, width), preferred_element_type=jnp.float32
    ).astype(jnp.bfloat16)
    return (result.reshape(tok_grp, feat_part), kv_pages)


def solution(mesh):
    return jax.shard_map(
        on_device,
        mesh=mesh,
        in_specs=(
            P("dp", "tensor"),
            P("dp", None),
            P("dp", None),
            P("dp", None),
            P(),
            P(None, "tensor"),
            P(),
            P(),
            P(),
            P("tensor", None),
            P(),
            P(None, "tensor"),
            P(None, "tensor"),
            P("tensor", None),
        ),
        out_specs=(P("dp", "tensor"), P("dp", None, "tensor")),
        check_vma=False,
    )
```

profile of v0, /device:TPU:65, one launch (start us, length us, event | category | flops | bytes accessed | tf_op | source)
XLA Modules:
  0.0 368.1 jit_solution(12057154090771228152)
XLA Ops:
  7.2 0.8 and_select_fusion.1
  8.0 0.7 fusion.57
  8.7 0.2 convert_reduce_fusion
  8.8 0.1 fusion.48
  8.9 0.1 select_reduce_fusion
  9.0 0.7 select_n.81
  9.8 8.4 %all-to-all-start = ((s32[32,1,2]{2,1,0:T(1,128)}), s32[32,1,2]{2,1,0:T(1,128)S(1)}, u32[]{:S(2)}, u32[]{:S(2)}) async-start(s32[32,1,2]{2,1,0:T(1,128)} %bitcast.5), calls=%async_computation | async-start | bytes 32768 | tf_op jit(solution)/shard_map/all_to_all | solution.py:92
  18.2 1.3 reshape.501
  19.5 1.5 convolution_convert_fusion.1
  21.0 2.5 reshape.502
  23.5 1.7 all-to-all-done
  25.2 6.3 %all-to-all-start.1 = ((bf16[32,2,8192]{2,1,0:T(2,128)(2,1)}), bf16[32,2,8192]{2,1,0:T(2,128)(2,1)}, u32[]{:S(2)}, u32[]{:S(2)}) async-start(bf16[32,2,8192]{2,1,0:T(2,128)(2,1)} %reshape.502), calls=%async_computation.1 | async-start | bytes 2097152 | tf_op jit(solution)/shard_map/all_to_all | solution.py:89
  31.5 0.0 all-gather.2.cloned.1.call-start
  31.6 0.5 broadcast.308
  32.1 0.7 reduce.8
  32.8 0.1 eq.55
  32.9 14.9 %all-to-all-done.1 = bf16[32,2,8192]{2,1,0:T(2,128)(2,1)} async-done(((bf16[32,2,8192]{2,1,0:T(2,128)(2,1)}), bf16[32,2,8192]{2,1,0:T(2,128)(2,1)}, u32[]{:S(2)}, u32[]{:S(2)}) %all-to-all-start.1) | async-done | bytes 1048608 | tf_op jit(solution)/shard_map/all_to_all | solution.py:89
  47.8 2.3 reshape.503
  50.1 1.5 convolution_convert_fusion.3
  51.6 1.0 reshape.504
  52.6 0.0 all-gather.2.cloned.1.call-update
  52.6 0.2 all-reduce.2.cloned.1.call-start
  52.9 0.5 slice.71
  54.1 0.1 add_select_fusion
  54.1 0.3 reduce-window.9
  54.4 0.1 slice.74
  54.6 0.1 slice_reduce_fusion
  54.7 0.1 fusion.55
  54.8 0.5 multiply_cosine_fusion
  55.3 1.0 compare_and_fusion
  56.3 0.5 fusion.10
  56.8 52.7 %all-gather.2.cloned.1.call-done = bf16[1024,2048]{1,0:T(8,128)(2,1)} async-done(((bf16[1024,256]{1,0:T(8,128)(2,1)}), bf16[1024,2048]{1,0:T(8,128)(2,1)}) %all-gather.2.cloned.1.call-update) | async-done | bytes 4194320 | tf_op jit(solution)/shard_map/all_gather | solution.py:101
  109.5 3.2 fusion.3
  112.8 0.2 copy-done.1
  113.0 2.6 fusion.19
  115.7 0.1 multiply_multiply_fusion.1
  115.8 0.6 fusion.34
  116.4 1.6 multiply_reduce_fusion
  118.0 0.1 multiply_multiply_fusion
  118.1 0.1 subtract_convert_fusion
  118.2 0.8 fusion.11
  119.0 1.1 fusion.7
  120.1 1.3 fusion.21
  121.4 0.7 convolution_convert_fusion.6
  122.2 0.3 copy-done.4
  122.5 3.3 convolution_convert_fusion.5
  125.7 0.0 all-reduce.2.cloned.1.call-update
  125.8 0.3 reduce-scatter.2.cloned.1.call-start
  126.0 116.0 %all-reduce.2.cloned.1.call-done = bf16[1024,2048]{1,0:T(8,128)(2,1)} async-done(((bf16[1024,2048]{1,0:T(8,128)(2,1)}), bf16[1024,2048]{1,0:T(8,128)(2,1)}) %all-reduce.2.cloned.1.call-update) | async-done | bytes 4194320 | tf_op jit(solution)/shard_map/psum | solution.py:154
  242.0 5.6 %fusion = (f32[1024]{0:T(1024)S(1)}, bf16[1024,2048]{1,0:T(8,128)(2,1)S(1)}) fusion(bf16[1024,2048]{1,0:T(8,128)(2,1)} %all-reduce.2.cloned.1.call-done, bf16[1024,2048]{1,0:T(8,128)(2,1)} %all-gather.2.cloned.1.call-done), kind=kLoop, calls=%fused_computation.10 | loop fusion | flops 14679040 | bytes 12587008 | tf_op jit(solution)/shard_map/reduce_sum | solution.py:18
  247.6 1.9 copy-done.2
  249.6 5.1 %fusion.13 = f32[1024,640]{1,0:T(8,128)} fusion(bf16[2048,640]{1,0:T(8,128)(2,1)S(1)} %copy-done.13, bf16[1024,2048]{1,0:T(8,128)(2,1)S(1)} %get-tuple-element.3, f32[2048]{0:T(1024)S(1)} %copy-done.17, f32[1024]{0:T(1024)S(1)} %add_rsqrt_fusion.1), kind=kOutput, calls=%fused_computation.31 | convolution fusion | flops 2692743168 | bytes 9449472 | tf_op jit(solution)/shard_map/dot_general | solution.py:159
  254.6 12.3 %convolution_convert_fusion.4 = bf16[1024,2048]{1,0:T(8,128)(2,1)} fusion(bf16[640,2048]{1,0:T(8,128)(2,1)S(1)} %copy-done, f32[1024,640]{1,0:T(8,128)} %fusion.13, bf16[2048,640]{1,0:T(8,128)(2,1)} %param.26, bf16[1024,2048]{1,0:T(8,128)(2,1)} %copy-done.2, f32[2048]{0:T(1024)S(1)} %copy-done.17, f32[1024]{0:T(1024)S(1)} %add_rsqrt_fusion.1), kind=kOutput, calls=%fused_computation.19 | convolution fusion | flops 5383127040 | bytes 16265216 | tf_op jit(solution)/shard_map/dot_general | solution.py:163
  267.0 59.3 %reduce-scatter.2.cloned.1.call-done = bf16[1024,256]{1,0:T(8,128)(2,1)} async-done(((bf16[1024,2048]{1,0:T(8,128)(2,1)}), bf16[1024,256]{1,0:T(8,128)(2,1)}) %reduce-scatter.2.cloned.1.call-update) | async-done | bytes 524304 | tf_op jit(solution)/shard_map/reduce_scatter | solution.py:162
  326.3 1.3 add_convert_fusion
  327.6 1.0 reshape.514
  328.7 2.5 convolution_convert_fusion
  331.2 2.5 reshape.515
  333.7 6.5 %all-to-all-start.2 = ((bf16[32,2,8192]{2,1,0:T(2,128)(2,1)}), bf16[32,2,8192]{2,1,0:T(2,128)(2,1)}, u32[]{:S(2)}, u32[]{:S(2)}) async-start(bf16[32,2,8192]{2,1,0:T(2,128)(2,1)} %reshape.515), calls=%async_computation.3 | async-start | bytes 2097152 | tf_op jit(solution)/shard_map/all_to_all | solution.py:173
  340.4 0.8 scatter_fusion
  341.2 15.5 %all-to-all-done.2 = bf16[32,2,8192]{2,1,0:T(2,128)(2,1)} async-done(((bf16[32,2,8192]{2,1,0:T(2,128)(2,1)}), bf16[32,2,8192]{2,1,0:T(2,128)(2,1)}, u32[]{:S(2)}, u32[]{:S(2)}) %all-to-all-start.2) | async-done | bytes 1048608 | tf_op jit(solution)/shard_map/all_to_all | solution.py:173
  356.6 2.3 reshape.516
  358.9 1.6 convolution_convert_fusion.2
  360.5 1.0 reshape.517
  (55 shorter events, 0.3 us)
Async XLA Ops:
  7.2 247.5 %copy-start = (bf16[640,2048]{1,0:T(8,128)(2,1)S(1)}, bf16[640,2048]{1,0:T(8,128)(2,1)}, u32[]{:S(2)}) copy-start(bf16[640,2048]{1,0:T(8,128)(2,1)} %param.27) | copy-start | bytes 7864324
  9.8 15.4 %all-to-all-start = ((s32[32,1,2]{2,1,0:T(1,128)}), s32[32,1,2]{2,1,0:T(1,128)S(1)}, u32[]{:S(2)}, u32[]{:S(2)}) async-start(s32[32,1,2]{2,1,0:T(1,128)} %bitcast.5), calls=%async_computation | async-start | bytes 32768 | tf_op jit(solution)/shard_map/all_to_all | solution.py:92
  23.5 29.4 %copy-start.10 = (s32[1,1024]{1,0:T(1,128)S(1)}, s32[1,1024]{1,0:T(1,128)}, u32[]{:S(2)}) copy-start(s32[1,1024]{1,0:T(1,128)} %param.16) | copy-start | bytes 12292
  25.2 22.6 %all-to-all-start.1 = ((bf16[32,2,8192]{2,1,0:T(2,128)(2,1)}), bf16[32,2,8192]{2,1,0:T(2,128)(2,1)}, u32[]{:S(2)}, u32[]{:S(2)}) async-start(bf16[32,2,8192]{2,1,0:T(2,128)(2,1)} %reshape.502), calls=%async_computation.1 | async-start | bytes 2097152 | tf_op jit(solution)/shard_map/all_to_all | solution.py:89
  31.5 78.0 %all-gather.2.cloned.1.call-start = ((), (), s32[]{:S(2)}) async-start(), calls=%async_computation.4 | async-start | bytes 4718592 | tf_op jit(solution)/shard_map/all_gather | solution.py:101
  50.1 62.7 %copy-start.15 = (f32[2048]{0:T(1024)S(1)}, f32[2048]{0:T(1024)}, u32[]{:S(2)}) copy-start(f32[2048]{0:T(1024)} %param.18) | copy-start | bytes 24580
  52.6 189.4 %all-reduce.2.cloned.1.call-start = ((), (), s32[]{:S(2)}) async-start(), calls=%async_computation.5 | async-start | bytes 8388608 | tf_op jit(solution)/shard_map/psum | solution.py:154
  109.5 3.4 copy-start.1
  113.0 2.7 copy-start.11
  113.0 3.4 copy-start.14
  113.0 3.4 copy-start.16
  116.4 2.6 copy-start.6
  116.4 2.6 copy-start.8
  116.4 1.6 copy-start.12
  116.4 1.8 copy-start.5
  121.4 1.0 copy-start.4
  125.8 123.8 %copy-start.17 = (f32[2048]{0:T(1024)S(1)}, f32[2048]{0:T(1024)}, u32[]{:S(2)}) copy-start(f32[2048]{0:T(1024)} %param.24) | copy-start | bytes 24580
  125.8 200.5 %reduce-scatter.2.cloned.1.call-start = ((), (), s32[]{:S(2)}) async-start(), calls=%async_computation.6 | async-start | bytes 4718592 | tf_op jit(solution)/shard_map/reduce_scatter | solution.py:162
  242.0 7.5 %copy-start.13 = (bf16[2048,640]{1,0:T(8,128)(2,1)S(1)}, bf16[2048,640]{1,0:T(8,128)(2,1)}, u32[]{:S(2)}) copy-start(bf16[2048,640]{1,0:T(8,128)(2,1)} %param.25) | copy-start | bytes 7864324
  247.6 1.9 copy-start.2
  267.0 73.3 %copy-start.18 = (s32[1,8]{1,0:T(1,128)S(1)}, s32[1,8]{1,0:T(1,128)}, u32[]{:S(2)}) copy-start(s32[1,8]{1,0:T(1,128)} %param.17) | copy-start | bytes 100
  267.0 73.3 %copy-start.7 = (bf16[1024,1,32]{0,2,1:T(8,128)(2,1)S(1)}, bf16[1024,1,32]{0,2,1:T(8,128)(2,1)}, u32[]{:S(2)}) copy-start(bf16[1024,1,32]{0,2,1:T(8,128)(2,1)} %copy-done.6) | copy-start | bytes 196612
  267.0 73.3 %copy-start.9 = (bf16[1024,1,32]{0,2,1:T(8,128)(2,1)S(1)}, bf16[1024,1,32]{0,2,1:T(8,128)(2,1)}, u32[]{:S(2)}) copy-start(bf16[1024,1,32]{0,2,1:T(8,128)(2,1)} %copy-done.8) | copy-start | bytes 196612
  333.7 22.9 %all-to-all-start.2 = ((bf16[32,2,8192]{2,1,0:T(2,128)(2,1)}), bf16[32,2,8192]{2,1,0:T(2,128)(2,1)}, u32[]{:S(2)}, u32[]{:S(2)}) async-start(bf16[32,2,8192]{2,1,0:T(2,128)(2,1)} %reshape.515), calls=%async_computation.3 | async-start | bytes 2097152 | tf_op jit(solution)/shard_map/all_to_all | solution.py:173
  341.2 20.4 %copy-start.3 = (bf16[8,128,64]{1,2,0:T(8,128)(2,1)}, bf16[8,128,64]{1,2,0:T(8,128)(2,1)S(1)}, u32[]{:S(2)}) copy-start(bf16[8,128,64]{1,2,0:T(8,128)(2,1)S(1)} %scatter_fusion) | copy-start | bytes 393220
Sparse Core Ops, SparseCore 0:
  52.8 56.6 all-gather.1
  125.9 116.0 all-reduce.1
  267.1 59.1 reduce-scatter.1
where the time goes:
time: 369 us; the launch traced here: 368 us
  waiting for transfers between devices  260 us (70%)
  matrix products  35.9 us (10%)
  starting transfers between devices  21.8 us (6%)
  local copies, waits for them, and re-layouts  19.4 us (5%)
  other arithmetic  16.1 us (4%)
  between operations  14.9 us (4%)
    psum x1, waiting for transfers between devices, on_device(): lax.psum(jnp.dot(attended, w_out, preferred_element_type=jnp.float32).ast...  116 us
    reduce_scatter x1, waiting for transfers between devices, on_device(): lax.psum_scatter(jnp.dot(hidden, w_down, preferred_element_type=jnp.float...  59.3 us
    all_gather x1, waiting for transfers between devices, on_device(): full = lax.all_gather(grouped, 'tensor', axis=1, tiled=True)  52.7 us
    all_to_all x1, waiting for transfers between devices, on_device(): lax.all_to_all(back.reshape(groups, MOST, width), 'dp', split_axis=0, con...  15.5 us
    all_to_all x1, waiting for transfers between devices, on_device(): lax.all_to_all(packed.reshape(groups, MOST, width), 'dp', split_axis=0, c...  14.9 us
    dot_general x1, matrix products, on_device(): jnp.dot(hidden, w_down, preferred_element_type=jnp.float32)  12.3 us
    reduce_sum x3, other arithmetic, rms_scale(): mean_sq = jnp.mean(values * values, axis=-1, keepdims=True)  8.85 us
    all_to_all x1, starting transfers between devices, on_device(): lax.all_to_all(slot_pos.reshape(groups, MOST), 'dp', split_axis=0, concat...  8.39 us
  transfers between devices with their start and end apart: 6, of which 6 were waited for; matrix products, arithmetic and copies ran while one was open for 3% of the time, Pallas kernels for 0%

commit v1 on v0

--- a/solution.py
+++ b/solution.py
@@ -3,6 +3,7 @@
 import jax.numpy as jnp
 from jax import lax
 from jax.sharding import PartitionSpec as P
+from jax.lax import all_gather
 
 HEAD = 64
 KVH = 4
@@ -151,8 +152,12 @@
         )
         outputs.append(mixed.astype(jnp.bfloat16).reshape(block, q_heads * HEAD))
     attended = jnp.concatenate(outputs, axis=0)
-    attn_sum = lax.psum(
-        jnp.dot(attended, w_out, preferred_element_type=jnp.float32).astype(jnp.bfloat16), "tensor"
+    attn_sum = jnp.sum(
+        all_gather(
+            jnp.dot(attended, w_out, preferred_element_type=jnp.float32).astype(jnp.bfloat16),
+            axis_name="tensor",
+        ),
+        axis=0,
     ).astype(jnp.float32)
     middle = (full.astype(jnp.float32) + attn_sum).astype(jnp.bfloat16)
     ffn_in = rms_scale(middle, ffn_gain).astype(jnp.bfloat16)

time: 369 us -> 560 us (1.52)
  waiting for transfers between devices: 260 us -> 437 us
  other arithmetic: 16.1 us -> 30.2 us
    all_gather x0 -> x1, waiting for transfers between devices: none -> 290 us  [on_device(): all_gather(jnp.dot(attended, w_out, preferred_element_type=jnp.float32).a...]
    psum x1 -> x0, waiting for transfers between devices: 116 us -> none  [on_device(): lax.psum(jnp.dot(attended, w_out, preferred_element_type=jnp.float32).ast...]
    reduce_sum x0 -> x1, other arithmetic: none -> 14.1 us  [on_device(): jnp.sum(all_gather(jnp.dot(attended, w_out, preferred_element_type=jnp.fl...]
  transfers between devices with their start and end apart: 6 -> 6, of which waited for: 6 -> 6; matrix products, arithmetic and copies ran while one was open for 3% -> 2% of each run, Pallas kernels for 0% -> 0%
where the time goes in v1:
time: 560 us
  waiting for transfers between devices  437 us (78%)
  matrix products  35.9 us (6%)
  other arithmetic  30.2 us (5%)
  starting transfers between devices  21.9 us (4%)
  local copies, waits for them, and re-layouts  19.4 us (3%)
  between operations  14.9 us (3%)
    all_gather x1, waiting for transfers between devices, on_device(): all_gather(jnp.dot(attended, w_out, preferred_element_type=jnp.float32).a...  290 us
    reduce_scatter x1, waiting for transfers between devices, on_device(): lax.psum_scatter(jnp.dot(hidden, w_down, preferred_element_type=jnp.float...  62.6 us
    all_gather x1, waiting for transfers between devices, on_device(): full = lax.all_gather(grouped, 'tensor', axis=1, tiled=True)  52.7 us
    all_to_all x1, waiting for transfers between devices, on_device(): lax.all_to_all(back.reshape(groups, MOST, width), 'dp', split_axis=0, con...  15.5 us
    all_to_all x1, waiting for transfers between devices, on_device(): lax.all_to_all(packed.reshape(groups, MOST, width), 'dp', split_axis=0, c...  14.9 us
    reduce_sum x1, other arithmetic, on_device(): jnp.sum(all_gather(jnp.dot(attended, w_out, preferred_element_type=jnp.fl...  14.1 us
    dot_general x1, matrix products, on_device(): jnp.dot(hidden, w_down, preferred_element_type=jnp.float32)  12.3 us
  transfers between devices with their start and end apart: 6, of which 6 were waited for; matrix products, arithmetic and copies ran while one was open for 2% of the time, Pallas kernels for 0%

profile of v1, /device:TPU:65, one launch (start us, length us, event | category | flops | bytes accessed | tf_op | source)
XLA Modules:
  0.0 559.6 jit_solution(12280431330435254490)
XLA Ops:
  7.2 0.8 and_select_fusion.1
  8.0 0.7 fusion.57
  8.7 0.2 convert_reduce_fusion
  8.8 0.1 fusion.48
  8.9 0.1 select_reduce_fusion
  9.0 0.7 select_n.81
  9.8 8.4 %all-to-all-start = ((s32[32,1,2]{2,1,0:T(1,128)}), s32[32,1,2]{2,1,0:T(1,128)S(1)}, u32[]{:S(2)}, u32[]{:S(2)}) async-start(s32[32,1,2]{2,1,0:T(1,128)} %bitcast.5), calls=%async_computation | async-start | bytes 32768 | tf_op jit(solution)/shard_map/all_to_all | solution.py:93
  18.2 1.3 reshape.501
  19.5 1.5 convolution_convert_fusion.1
  21.0 2.5 reshape.502
  23.5 1.7 all-to-all-done
  25.2 6.3 %all-to-all-start.1 = ((bf16[32,2,8192]{2,1,0:T(2,128)(2,1)}), bf16[32,2,8192]{2,1,0:T(2,128)(2,1)}, u32[]{:S(2)}, u32[]{:S(2)}) async-start(bf16[32,2,8192]{2,1,0:T(2,128)(2,1)} %reshape.502), calls=%async_computation.1 | async-start | bytes 2097152 | tf_op jit(solution)/shard_map/all_to_all | solution.py:90
  31.5 0.0 all-gather.4.cloned.1.call-start
  31.6 0.5 broadcast.308
  32.1 0.7 reduce.9
  32.8 0.1 eq.55
  32.9 14.9 %all-to-all-done.1 = bf16[32,2,8192]{2,1,0:T(2,128)(2,1)} async-done(((bf16[32,2,8192]{2,1,0:T(2,128)(2,1)}), bf16[32,2,8192]{2,1,0:T(2,128)(2,1)}, u32[]{:S(2)}, u32[]{:S(2)}) %all-to-all-start.1) | async-done | bytes 1048608 | tf_op jit(solution)/shard_map/all_to_all | solution.py:90
  47.8 2.3 reshape.503
  50.1 1.5 convolution_convert_fusion.3
  51.6 1.0 reshape.504
  52.6 0.0 all-gather.4.cloned.1.call-update
  52.6 0.2 all-gather.6.cloned.1.call-start
  52.9 0.5 slice.71
  54.1 0.1 add_select_fusion
  54.1 0.3 reduce-window.9
  54.4 0.1 slice.74
  54.6 0.1 slice_reduce_fusion
  54.7 0.1 fusion.55
  54.8 0.5 multiply_cosine_fusion
  55.3 1.0 compare_and_fusion
  56.3 0.5 fusion.10
  56.8 52.7 %all-gather.4.cloned.1.call-done = bf16[1024,2048]{1,0:T(8,128)(2,1)} async-done(((bf16[1024,256]{1,0:T(8,128)(2,1)}), bf16[1024,2048]{1,0:T(8,128)(2,1)}) %all-gather.4.cloned.1.call-update) | async-done | bytes 4194320 | tf_op jit(solution)/shard_map/all_gather | solution.py:102
  109.5 3.2 fusion.3
  112.8 0.2 copy-done.1
  113.0 2.6 fusion.19
  115.7 0.1 multiply_multiply_fusion.1
  115.8 0.6 fusion.34
  116.4 1.6 multiply_reduce_fusion
  118.0 0.1 multiply_multiply_fusion
  118.1 0.1 subtract_convert_fusion
  118.2 0.8 fusion.11
  119.0 1.1 fusion.7
  120.1 1.3 fusion.21
  121.4 0.7 convolution_convert_fusion.6
  122.2 0.3 copy-done.4
  122.5 3.2 convolution_convert_fusion.5
  125.7 0.3 reduce-scatter.2.cloned.1.call-start
  126.0 290.0 %all-gather.6.cloned.1.call-done = bf16[8192,2048]{1,0:T(8,128)(2,1)} async-done(((bf16[1024,2048]{1,0:T(8,128)(2,1)}), bf16[8192,2048]{1,0:T(8,128)(2,1)}) %all-gather.6.cloned.1.call-update) | async-done | bytes 33554448 | tf_op jit(solution)/shard_map/all_gather | solution.py:156
  416.0 14.1 %reduce_sum.94 = bf16[1024,2048]{1,0:T(8,128)(2,1)} reduce(bf16[8,1024,2048]{2,1,0:T(8,128)(2,1)} %bitcast.134, bf16[]{:T(256)} %constant.101.clone.1), dimensions={0}, to_apply=%region_10.11 | reduce | flops 14680064 | bytes 37748736 | tf_op jit(solution)/shard_map/reduce_sum | solution.py:155
  430.1 5.6 %fusion = (f32[1024]{0:T(1024)S(1)}, bf16[1024,2048]{1,0:T(8,128)(2,1)S(1)}) fusion(bf16[1024,2048]{1,0:T(8,128)(2,1)} %reduce_sum.94, bf16[1024,2048]{1,0:T(8,128)(2,1)} %all-gather.4.cloned.1.call-done), kind=kLoop, calls=%fused_computation.10 | loop fusion | flops 14679040 | bytes 12587008 | tf_op jit(solution)/shard_map/reduce_sum | solution.py:19
  435.7 1.9 copy-done.2
  437.6 5.1 fusion.13
  442.7 12.3 %convolution_convert_fusion.4 = bf16[1024,2048]{1,0:T(8,128)(2,1)} fusion(bf16[640,2048]{1,0:T(8,128)(2,1)S(1)} %copy-done, f32[1024,640]{1,0:T(8,128)} %fusion.13, bf16[2048,640]{1,0:T(8,128)(2,1)} %param.26, bf16[1024,2048]{1,0:T(8,128)(2,1)} %copy-done.2, f32[2048]{0:T(1024)S(1)} %copy-done.17, f32[1024]{0:T(1024)S(1)} %add_rsqrt_fusion.1), kind=kOutput, calls=%fused_computation.19 | convolution fusion | flops 5383127040 | bytes 16265216 | tf_op jit(solution)/shard_map/dot_general | solution.py:168
  455.1 62.6 %reduce-scatter.2.cloned.1.call-done = bf16[1024,256]{1,0:T(8,128)(2,1)} async-done(((bf16[1024,2048]{1,0:T(8,128)(2,1)}), bf16[1024,256]{1,0:T(8,128)(2,1)}) %reduce-scatter.2.cloned.1.call-update) | async-done | bytes 524304 | tf_op jit(solution)/shard_map/reduce_scatter | solution.py:167
  517.8 1.3 add_convert_fusion
  519.1 1.0 reshape.514
  520.1 2.5 convolution_convert_fusion
  522.7 2.5 reshape.515
  525.2 6.6 %all-to-all-start.2 = ((bf16[32,2,8192]{2,1,0:T(2,128)(2,1)}), bf16[32,2,8192]{2,1,0:T(2,128)(2,1)}, u32[]{:S(2)}, u32[]{:S(2)}) async-start(bf16[32,2,8192]{2,1,0:T(2,128)(2,1)} %reshape.515), calls=%async_computation.3 | async-start | bytes 2097152 | tf_op jit(solution)/shard_map/all_to_all | solution.py:178
  532.0 0.8 scatter_fusion
  532.8 15.5 %all-to-all-done.2 = bf16[32,2,8192]{2,1,0:T(2,128)(2,1)} async-done(((bf16[32,2,8192]{2,1,0:T(2,128)(2,1)}), bf16[32,2,8192]{2,1,0:T(2,128)(2,1)}, u32[]{:S(2)}, u32[]{:S(2)}) %all-to-all-start.2) | async-done | bytes 1048608 | tf_op jit(solution)/shard_map/all_to_all | solution.py:178
  548.2 2.3 reshape.516
  550.5 1.6 convolution_convert_fusion.2
  552.1 1.0 reshape.517
  (56 shorter events, 0.3 us)
Async XLA Ops:
  7.2 435.6 %copy-start = (bf16[640,2048]{1,0:T(8,128)(2,1)S(1)}, bf16[640,2048]{1,0:T(8,128)(2,1)}, u32[]{:S(2)}) copy-start(bf16[640,2048]{1,0:T(8,128)(2,1)} %param.27) | copy-start | bytes 7864324
  9.8 15.4 %all-to-all-start = ((s32[32,1,2]{2,1,0:T(1,128)}), s32[32,1,2]{2,1,0:T(1,128)S(1)}, u32[]{:S(2)}, u32[]{:S(2)}) async-start(s32[32,1,2]{2,1,0:T(1,128)} %bitcast.5), calls=%async_computation | async-start | bytes 32768 | tf_op jit(solution)/shard_map/all_to_all | solution.py:93
  23.5 29.4 %copy-start.10 = (s32[1,1024]{1,0:T(1,128)S(1)}, s32[1,1024]{1,0:T(1,128)}, u32[]{:S(2)}) copy-start(s32[1,1024]{1,0:T(1,128)} %param.16) | copy-start | bytes 12292
  25.2 22.6 %all-to-all-start.1 = ((bf16[32,2,8192]{2,1,0:T(2,128)(2,1)}), bf16[32,2,8192]{2,1,0:T(2,128)(2,1)}, u32[]{:S(2)}, u32[]{:S(2)}) async-start(bf16[32,2,8192]{2,1,0:T(2,128)(2,1)} %reshape.502), calls=%async_computation.1 | async-start | bytes 2097152 | tf_op jit(solution)/shard_map/all_to_all | solution.py:90
  31.5 78.0 %all-gather.4.cloned.1.call-start = ((), (), s32[]{:S(2)}) async-start(), calls=%async_computation.4 | async-start | bytes 4718592 | tf_op jit(solution)/shard_map/all_gather | solution.py:102
  50.1 62.7 %copy-start.15 = (f32[2048]{0:T(1024)S(1)}, f32[2048]{0:T(1024)}, u32[]{:S(2)}) copy-start(f32[2048]{0:T(1024)} %param.18) | copy-start | bytes 24580
  52.6 363.3 %all-gather.6.cloned.1.call-start = ((), (), s32[]{:S(2)}) async-start(), calls=%async_computation.6 | async-start | bytes 37748736 | tf_op jit(solution)/shard_map/all_gather | solution.py:156
  109.5 3.4 copy-start.1
  113.0 2.7 copy-start.11
  113.0 3.4 copy-start.14
  113.0 3.4 copy-start.16
  116.4 2.6 copy-start.6
  116.4 2.6 copy-start.8
  116.4 1.6 copy-start.12
  116.4 1.8 copy-start.5
  121.4 1.0 copy-start.4
  125.7 392.1 %reduce-scatter.2.cloned.1.call-start = ((), (), s32[]{:S(2)}) async-start(), calls=%async_computation.5 | async-start | bytes 4718592 | tf_op jit(solution)/shard_map/reduce_scatter | solution.py:167
  430.1 7.5 %copy-start.13 = (bf16[2048,640]{1,0:T(8,128)(2,1)S(1)}, bf16[2048,640]{1,0:T(8,128)(2,1)}, u32[]{:S(2)}) copy-start(bf16[2048,640]{1,0:T(8,128)(2,1)} %param.25) | copy-start | bytes 7864324
  430.1 7.5 %copy-start.17 = (f32[2048]{0:T(1024)S(1)}, f32[2048]{0:T(1024)}, u32[]{:S(2)}) copy-start(f32[2048]{0:T(1024)} %param.24) | copy-start | bytes 24580
  435.7 1.9 copy-start.2
  455.1 76.8 %copy-start.18 = (s32[1,8]{1,0:T(1,128)S(1)}, s32[1,8]{1,0:T(1,128)}, u32[]{:S(2)}) copy-start(s32[1,8]{1,0:T(1,128)} %param.17) | copy-start | bytes 100
  455.1 76.8 %copy-start.7 = (bf16[1024,1,32]{0,2,1:T(8,128)(2,1)S(1)}, bf16[1024,1,32]{0,2,1:T(8,128)(2,1)}, u32[]{:S(2)}) copy-start(bf16[1024,1,32]{0,2,1:T(8,128)(2,1)} %copy-done.6) | copy-start | bytes 196612
  455.1 76.8 %copy-start.9 = (bf16[1024,1,32]{0,2,1:T(8,128)(2,1)S(1)}, bf16[1024,1,32]{0,2,1:T(8,128)(2,1)}, u32[]{:S(2)}) copy-start(bf16[1024,1,32]{0,2,1:T(8,128)(2,1)} %copy-done.8) | copy-start | bytes 196612
  525.2 23.0 %all-to-all-start.2 = ((bf16[32,2,8192]{2,1,0:T(2,128)(2,1)}), bf16[32,2,8192]{2,1,0:T(2,128)(2,1)}, u32[]{:S(2)}, u32[]{:S(2)}) async-start(bf16[32,2,8192]{2,1,0:T(2,128)(2,1)} %reshape.515), calls=%async_computation.3 | async-start | bytes 2097152 | tf_op jit(solution)/shard_map/all_to_all | solution.py:178
  532.8 20.4 %copy-start.3 = (bf16[8,128,64]{1,2,0:T(8,128)(2,1)}, bf16[8,128,64]{1,2,0:T(8,128)(2,1)S(1)}, u32[]{:S(2)}) copy-start(bf16[8,128,64]{1,2,0:T(8,128)(2,1)S(1)} %scatter_fusion) | copy-start | bytes 393220
Sparse Core Ops, SparseCore 0:
  52.8 56.6 all-gather.3
  125.8 290.0 all-gather.5
  455.2 62.5 reduce-scatter.1
